TPU v7x, 512 devices: a whole 4x4x16 slice. The times are simulated.
512 devices in a mesh: ctx: 64 (over z_hi, y, x), ch: 8 (over z_lo, core).
Axes of the slice: x: 4, y: 4, z: 16 (z_hi: 4, z_lo: 4; z = z_hi * 4 + z_lo), core: 2. Of those that a mesh axis runs over, the one named last changes fastest.
Arguments:
- first_gate: bfloat16 [8192, 8192], P('ctx', 'ch'), may hold values from -6 to 6
- second_gate: bfloat16 [8192, 8192], P('ctx', 'ch'), may hold values from -6 to 6
- output_gate: bfloat16 [8192, 8192], P('ctx', 'ch'), may hold values from -6 to 6
- values: bfloat16 [8192, 8192], P('ctx', 'ch'), may hold values from -6 to 6
- cotangent: bfloat16 [8192, 8192], P('ctx', 'ch'), may hold values from -6 to 6
- medium_filter: bfloat16 [128, 512], P(None, 'ch'), may hold values from -0.5 to 0.5
- long_filter: bfloat16 [8192, 512], P('ctx', 'ch'), may hold values from -0.044194174 to 0.044194174
Outputs:
- grad_first: bfloat16 [8192, 8192], P('ctx', 'ch')
- grad_second: bfloat16 [8192, 8192], P('ctx', 'ch')
- grad_output_gate: bfloat16 [8192, 8192], P('ctx', 'ch')
- grad_values: bfloat16 [8192, 8192], P('ctx', 'ch')
- grad_medium: float32 [128, 512], P(None, 'ch')
- grad_long: bfloat16 [8192, 512], P('ctx', 'ch')
- filter_rms: float32 [], replicated
All inputs are finite; a program needn't handle non-finite values.
Results may differ from a plain program's by a relative error of at most 0.011.
Values may be sent and summed in bfloat16 or wider, within the bound.
No kernel may reach another device: no remote copies, remote signals or barrier semaphores. Data moves between devices by JAX's collectives and lax.ppermute only.
A program may use at most 64 MiB of HBM per device.

v0:
```python
import math
import jax
import jax.numpy as jnp
from jax import lax
from jax.sharding import PartitionSpec as P

radix_cols = 128
block_limit = 64
highest = lax.Precision.HIGH
wide_type = jnp.float32
narrow_type = jnp.bfloat16


def passed_along(array, axis, by):
    peers = lax.axis_size(axis)
    pairs = [(i, i + by) for i in range(peers) if 0 <= i + by < peers]
    return lax.ppermute(array, axis, pairs)


def band_table(filt, block_rows, flipped):
    tap_count, group_count = filt.shape
    window_rows = block_rows + tap_count - 1
    leading = filt[::-1] if flipped else filt
    padded = jnp.concatenate([leading.T, jnp.zeros((group_count, block_rows), filt.dtype)], axis=1)
    tiled = jnp.broadcast_to(padded[:, None, :], (group_count, block_rows, window_rows + 1))
    tiled = tiled.reshape(group_count, block_rows * (window_rows + 1))
    return tiled[:, : block_rows * window_rows].reshape(group_count, block_rows, window_rows)


def windows_of(extended, block_rows, block_count, window_rows):
    return jnp.stack(
        [
            extended[number * block_rows : number * block_rows + window_rows]
            for number in range(block_count)
        ]
    )


def phase_table(row_count, col_count, period):
    row_ids = lax.broadcasted_iota(jnp.int32, (row_count, col_count), 0)
    col_ids = lax.broadcasted_iota(jnp.int32, (row_count, col_count), 1)
    angle = (row_ids * col_ids % period).astype(wide_type) * (2.0 * math.pi / period)
    return (jnp.cos(angle), jnp.sin(angle))


def forward_dft(signal, tables):
    outer_table, cos_twist, sin_twist, forward_inner, inverse_inner = tables
    outer = jnp.einsum("kna,nmb->mkab", outer_table, signal, precision=highest)
    real_part = outer[:, 0]
    imag_part = outer[:, 1]
    twisted = jnp.stack(
        [
            real_part * cos_twist + imag_part * sin_twist,
            imag_part * cos_twist - real_part * sin_twist,
        ],
        axis=1,
    )
    return jnp.einsum("mkab,kjbq->mjaq", twisted, forward_inner, precision=highest)


def inverse_dft(spectrum, tables, total_len):
    outer_table, cos_twist, sin_twist, forward_inner, inverse_inner = tables
    inner = jnp.einsum("mkab,kjbq->mjaq", spectrum, inverse_inner, precision=highest)
    real_part = inner[:, 0]
    imag_part = inner[:, 1]
    twisted = jnp.stack(
        [
            real_part * cos_twist - imag_part * sin_twist,
            imag_part * cos_twist + real_part * sin_twist,
        ],
        axis=1,
    )
    signal = jnp.einsum("kna,mkab->nmb", outer_table, twisted, precision=highest)
    return signal / total_len


def split_wide(value):
    high = value.astype(narrow_type)
    low = (value - high.astype(wide_type)).astype(narrow_type)
    return (high, low)


def joined_wide(high, low):
    return high.astype(wide_type) + low.astype(wide_type)


def medium_bands(filt):
    tap_count, item_count = filt.shape
    bands = band_table(filt, tap_count, False)
    near = bands[:, :, :tap_count]
    far = jnp.concatenate(
        [bands[:, :, tap_count:], jnp.zeros((item_count, tap_count, 1), filt.dtype)], axis=2
    )
    return (near, far)


def channel_work(pieces, filt):
    gated_part, grad_part, gate_part, filter_part = pieces
    half_rows = gated_part.shape[0]
    chan_total = gated_part.shape[1]
    item_count = filter_part.shape[1]
    group_size = chan_total // item_count
    seq_len = half_rows * radix_cols
    full_rows = 2 * half_rows
    total_len = 2 * seq_len
    scale = 1.0 / math.sqrt(seq_len * group_size)
    by_item = (half_rows, item_count, group_size, radix_cols)
    near, far = medium_bands(filt)
    gated_items = gated_part.reshape(by_item)
    gated_prev = jnp.concatenate([jnp.zeros_like(gated_items[:1]), gated_items[:-1]], axis=0)
    mixed = (
        jnp.einsum("ngcs,gsr->ngcr", gated_items, near, preferred_element_type=wide_type)
        + jnp.einsum("ngcs,gsr->ngcr", gated_prev, far, preferred_element_type=wide_type)
    ).reshape(half_rows, chan_total, radix_cols)
    gate_wide = gate_part.astype(wide_type)
    carried = (gate_wide * mixed).astype(narrow_type)
    cos_outer, sin_outer = phase_table(half_rows, full_rows, full_rows)
    cos_twist, sin_twist = phase_table(full_rows, radix_cols, total_len)
    cos_inner, sin_inner = phase_table(radix_cols, radix_cols, radix_cols)
    outer_table = jnp.stack([cos_outer, -sin_outer])
    forward_inner = jnp.stack(
        [jnp.stack([cos_inner, -sin_inner]), jnp.stack([sin_inner, cos_inner])]
    )
    inverse_inner = jnp.stack(
        [jnp.stack([cos_inner, sin_inner]), jnp.stack([-sin_inner, cos_inner])]
    )
    tables = (outer_table, cos_twist, sin_twist, forward_inner, inverse_inner)
    shaped = (item_count, group_size, 2, full_rows, radix_cols)
    flat_shape = (chan_total, 2, full_rows, radix_cols)
    signals = jnp.concatenate([carried, grad_part], axis=1).astype(wide_type)
    both_specs = forward_dft(signals, tables)
    gated_spec = both_specs[:chan_total].reshape(shaped)
    inner_spec = both_specs[chan_total:].reshape(shaped)
    filt_spec = forward_dft(filter_part.astype(wide_type), tables)[:, None]
    gated_re = gated_spec[:, :, 0]
    gated_im = gated_spec[:, :, 1]
    inner_re = inner_spec[:, :, 0]
    inner_im = inner_spec[:, :, 1]
    filt_re = filt_spec[:, :, 0]
    filt_im = filt_spec[:, :, 1]
    conv_spec = jnp.stack(
        [gated_re * filt_re - gated_im * filt_im, gated_re * filt_im + gated_im * filt_re], axis=2
    )
    back_spec = jnp.stack(
        [inner_re * filt_re + inner_im * filt_im, inner_im * filt_re - inner_re * filt_im], axis=2
    )
    corr_spec = jnp.stack(
        [inner_re * gated_re + inner_im * gated_im, inner_im * gated_re - inner_re * gated_im],
        axis=2,
    )
    signals_back = inverse_dft(
        jnp.concatenate([conv_spec.reshape(flat_shape), back_spec.reshape(flat_shape)], axis=0),
        tables,
        total_len,
    )
    second_mix = signals_back[:, :chan_total].astype(narrow_type)
    grad_carried = signals_back[:, chan_total:].astype(narrow_type).astype(wide_type)
    summed = jnp.sum(corr_spec, axis=1)
    lagged = (inverse_dft(summed, tables, total_len) * scale).astype(narrow_type)
    grad_second = (grad_carried * mixed).astype(narrow_type)
    grad_mixed = (grad_carried * gate_wide).astype(narrow_type)
    mixed_items = grad_mixed.reshape(by_item)
    mixed_next = jnp.concatenate([mixed_items[1:], jnp.zeros_like(mixed_items[:1])], axis=0)
    grad_gated = (
        jnp.einsum("ngcs,grs->ngcr", mixed_items, near, preferred_element_type=wide_type)
        + jnp.einsum("ngcs,grs->ngcr", mixed_next, far, preferred_element_type=wide_type)
    ).reshape(half_rows, chan_total, radix_cols)
    tap_count = filt.shape[0]
    own_lags = jnp.einsum(
        "ngcs,ngcr->gsr", gated_items, mixed_items, preferred_element_type=wide_type
    )
    prev_lags = jnp.einsum(
        "ngcs,ngcr->gsr", gated_prev, mixed_items, preferred_element_type=wide_type
    )
    cube = (tap_count, tap_count, tap_count)
    lag_of = lax.broadcasted_iota(jnp.int32, cube, 2) - lax.broadcasted_iota(jnp.int32, cube, 1)
    lag_ids = lax.broadcasted_iota(jnp.int32, cube, 0)
    on_own = (lag_of == lag_ids)[None]
    on_prev = (lag_of + tap_count == lag_ids)[None]
    grad_medium = (
        jnp.sum(
            jnp.where(on_own, own_lags[:, None], 0.0) + jnp.where(on_prev, prev_lags[:, None], 0.0),
            axis=(2, 3),
        )
        * scale
    )
    squares = jnp.sum(jnp.square(lagged.astype(wide_type))) + jnp.sum(grad_medium * grad_medium)
    squares = lax.psum(squares, "ch")
    medium_high, medium_low = split_wide(grad_medium)
    squares_high, squares_low = split_wide(squares)
    squares_row = jnp.concatenate(
        [
            squares_high.reshape(1, 1),
            squares_low.reshape(1, 1),
            jnp.zeros((1, radix_cols - 2), narrow_type),
        ],
        axis=1,
    )
    shared = jnp.concatenate([medium_high, medium_low, squares_row], axis=0)
    shared = jnp.broadcast_to(shared[None], (half_rows,) + shared.shape)
    return jnp.concatenate(
        [second_mix, grad_second, grad_gated.astype(narrow_type), lagged, shared], axis=1
    )


def body(first_gate, second_gate, output_gate, values, cotangent, medium_filter, long_filter):
    tok_rows, chan_local = first_gate.shape
    tap_count, local_groups = medium_filter.shape
    group_size = chan_local // local_groups
    ctx_devices = lax.axis_size("ctx")
    ctx_groups = local_groups // ctx_devices
    chan_share = ctx_groups * group_size
    first_wide = first_gate.astype(wide_type)
    values_wide = values.astype(wide_type)
    cotangent_wide = cotangent.astype(wide_type)
    gated_input = (first_wide * values_wide).astype(narrow_type)
    grad_inner = (cotangent_wide * output_gate.astype(wide_type)).astype(narrow_type)

    def token_major(matrix):
        return matrix.T.reshape(ctx_devices, -1, tok_rows)

    outbound = jnp.concatenate(
        [
            token_major(gated_input),
            token_major(grad_inner),
            token_major(second_gate),
            token_major(long_filter),
        ],
        axis=1,
    )
    arrived = lax.all_to_all(outbound, "ctx", 0, 0, tiled=True)
    own_filter = lax.dynamic_slice_in_dim(
        medium_filter, lax.axis_index("ctx") * ctx_groups, ctx_groups, axis=1
    )
    returned = channel_work(
        (
            arrived[:, :chan_share],
            arrived[:, chan_share : 2 * chan_share],
            arrived[:, 2 * chan_share : 3 * chan_share],
            arrived[:, 3 * chan_share :],
        ),
        own_filter,
    )
    back = lax.all_to_all(returned, "ctx", 0, 0, tiled=True)

    def token_rows(start, count):
        return back[:, start : start + count].reshape(ctx_devices * count, tok_rows).T

    second_mix = token_rows(0, chan_share)
    grad_second = token_rows(chan_share, chan_share)
    grad_gated = token_rows(2 * chan_share, chan_share).astype(wide_type)
    grad_long = token_rows(3 * chan_share, ctx_groups)
    grad_medium = joined_wide(
        token_rows(3 * chan_share + ctx_groups, ctx_groups),
        token_rows(3 * chan_share + 2 * ctx_groups, ctx_groups),
    )
    squares_row = back[:, 3 * chan_share + 3 * ctx_groups]
    total_squares = jnp.sum(joined_wide(squares_row[:, 0], squares_row[:, 1]))
    grad_output_gate = (cotangent_wide * second_mix.astype(wide_type)).astype(narrow_type)
    grad_first = (grad_gated * values_wide).astype(narrow_type)
    grad_values = (grad_gated * first_wide).astype(narrow_type)
    entries = (tok_rows * ctx_devices + tap_count) * local_groups * lax.axis_size("ch")
    filter_rms = jnp.sqrt(total_squares / entries)
    return (
        grad_first,
        grad_second,
        grad_output_gate,
        grad_values,
        grad_medium,
        grad_long,
        filter_rms,
    )


def solution(mesh):
    return jax.shard_map(
        body,
        mesh=mesh,
        in_specs=(
            P("ctx", "ch"),
            P("ctx", "ch"),
            P("ctx", "ch"),
            P("ctx", "ch"),
            P("ctx", "ch"),
            P(None, "ch"),
            P("ctx", "ch"),
        ),
        out_specs=(
            P("ctx", "ch"),
            P("ctx", "ch"),
            P("ctx", "ch"),
            P("ctx", "ch"),
            P(None, "ch"),
            P("ctx", "ch"),
            P(),
        ),
        check_vma=False,
    )
```

profile of v0, /device:TPU:1, one launch (start us, length us, event | category | flops | bytes accessed | tf_op | source)
XLA Modules:
  0.0 178.5 jit_solution(15019823692535973274)
XLA Ops:
  0.7 1.2 copy.100
  1.8 1.1 copy.99
  3.0 1.1 copy.101
  4.1 1.1 copy.102
  5.6 1.0 pad_maximum_fusion
  6.6 21.7 %all-to-all-start = ((bf16[64,49,128]{2,1,0:T(8,128)(2,1)}), bf16[64,49,128]{2,1,0:T(8,128)(2,1)S(1)}, u32[]{:S(2)}, u32[]{:S(2)}) async-start(bf16[64,49,128]{2,1,0:T(8,128)(2,1)} %pad_maximum_fusion), calls=%async_computation | async-start | bytes 1835008 | tf_op jit(solution)/shard_map/all_to_all | solution.py:231
  28.5 0.4 slice_reduce_fusion
  28.9 0.3 reshape.489
  30.3 39.9 %all-to-all-done = bf16[64,49,128]{2,1,0:T(8,128)(2,1)S(1)} async-done(((bf16[64,49,128]{2,1,0:T(8,128)(2,1)}), bf16[64,49,128]{2,1,0:T(8,128)(2,1)S(1)}, u32[]{:S(2)}, u32[]{:S(2)}) %all-to-all-start) | async-done | bytes 802848 | tf_op jit(solution)/shard_map/all_to_all | solution.py:231
  70.9 1.3 convolution_bitcast_fusion
  72.2 0.8 multiply_add_fusion.1
  73.1 2.1 %fusion.12 = f32[32,2,128,128]{2,3,0,1:T(8,128)S(1)} fusion(f32[32,1,128,128]{2,3,1,0:T(8,128)S(1)} %get-tuple-element.38, f32[32,1,128,128]{2,3,1,0:T(8,128)S(1)} %get-tuple-element.37, f32[1,2,128,128]{2,3,0,1:T(8,128)S(1)} %get-tuple-element.64, f32[1,2,128,128]{2,3,0,1:T(8,128)S(1)} %get-tuple-element.71), kind=kOutput, calls=%fused_computation.16 | convolution fusion | flops 1611726848 | bytes 8650752 | tf_op jit(solution)/shard_map/mkab,kjbq->mjaq/dot_general | solution.py:58
  75.7 0.3 multiply_add_fusion.6
  76.0 0.3 convolution_bitcast_fusion.2
  76.3 1.2 multiply_add_fusion.2
  77.8 2.1 %fusion.9 = f32[32,2,128,128]{2,3,1,0:T(8,128)S(1)} fusion(f32[16,2,128,128]{2,3,0,1:T(8,128)S(1)} %maximum_bitcast_fusion.6, f32[16,2,128,128]{2,3,0,1:T(8,128)S(1)} %maximum_bitcast_fusion.5, f32[1,2,128,128]{2,3,1,0:T(8,128)S(1)} %get-tuple-element.72, f32[1,2,128,128]{2,3,1,0:T(8,128)S(1)} %get-tuple-element.63), kind=kOutput, calls=%fused_computation.15 | convolution fusion | flops 1611726848 | bytes 8650752 | tf_op jit(solution)/shard_map/mkab,kjbq->mjaq/dot_general | solution.py:63
  79.9 0.8 multiply_subtract_fusion
  80.7 2.2 %fusion.19 = bf16[64,32,128]{2,0,1:T(8,128)(2,1)S(1)} fusion(f32[32,1,128,128]{2,3,1,0:T(8,128)S(1)} %get-tuple-element.36, f32[32,1,128,128]{2,3,1,0:T(8,128)S(1)} %get-tuple-element.35, f32[1,64,128]{2,1,0:T(8,128)S(1)} %get-tuple-element.79, f32[1,64,128]{2,1,0:T(8,128)S(1)} %get-tuple-element.80), kind=kOutput, calls=%fused_computation.29 | convolution fusion | flops 404242432 | bytes 4784128 | tf_op jit(solution)/shard_map/kna,mkab->nmb/dot_general | solution.py:73
  83.9 2.5 %add_reduce_fusion = f32[128]{0:T(128)S(1)} fusion(f32[128,128]{1,0:T(8,128)S(1)} %convolution_bitcast_fusion.4, f32[128,128]{1,0:T(8,128)S(1)} %convolution_bitcast_fusion.5), kind=kLoop, calls=%fused_computation | loop fusion | flops 16777088 | bytes 131584 | tf_op jit(solution)/shard_map/reduce_sum | solution.py:181
  86.4 0.6 bitcast_convert_fusion
  87.4 0.3 multiply_subtract_fusion.5
  88.3 0.6 multiply_reduce_fusion
  90.2 21.0 %psum.7 = f32[]{:T(128)} all-reduce(f32[]{:T(128)S(6)} %add.226), channel_id=1, replica_groups=mesh['ctx'=64,'ch'=8] {'ch'}, use_global_device_ids=true, to_apply=%region_4.5 | all-reduce | flops 1 | bytes 8 | tf_op jit(solution)/shard_map/psum | solution.py:188
  112.6 0.6 copy.118
  113.2 57.7 %all_to_all.10 = bf16[64,52,128]{2,1,0:T(8,128)(2,1)S(1)} all-to-all(bf16[64,52,128]{2,1,0:T(8,128)(2,1)S(1)} %copy.118), channel_id=1, replica_groups=mesh['ctx'=64,'ch'=8] {'ctx'}, dimensions={0} | all-to-all | bytes 1703936 | tf_op jit(solution)/shard_map/all_to_all | solution.py:244
  171.2 0.8 copy.121
  172.0 0.8 copy.124
  173.0 0.8 copy.123
  173.8 0.8 copy.122
  174.7 0.7 add_reduce_fusion.1
  176.1 0.6 copy.173
  176.7 0.7 fusion.83
  (52 shorter events, 5.5 us)
Async XLA Ops:
  0.6 27.7 %copy-start = (bf16[128,64]{0,1:T(8,128)(2,1)S(1)}, bf16[128,64]{0,1:T(8,128)(2,1)}, u32[]{:S(2)}) copy-start(bf16[128,64]{0,1:T(8,128)(2,1)} %param.12) | copy-start | bytes 49156
  0.6 4.6 %copy-start.1 = (bf16[128,1024]{1,0:T(8,128)(2,1)S(1)}, bf16[128,1024]{1,0:T(8,128)(2,1)}, u32[]{:S(2)}) copy-start(bf16[128,1024]{1,0:T(8,128)(2,1)} %param.8) | copy-start | bytes 786436
  0.7 4.7 %copy-start.2 = (bf16[128,64]{0,1:T(8,128)(2,1)S(1)}, bf16[128,64]{0,1:T(8,128)(2,1)}, u32[]{:S(2)}) copy-start(bf16[128,64]{0,1:T(8,128)(2,1)} %param.13) | copy-start | bytes 49156
  6.6 63.5 %all-to-all-start = ((bf16[64,49,128]{2,1,0:T(8,128)(2,1)}), bf16[64,49,128]{2,1,0:T(8,128)(2,1)S(1)}, u32[]{:S(2)}, u32[]{:S(2)}) async-start(bf16[64,49,128]{2,1,0:T(8,128)(2,1)} %pad_maximum_fusion), calls=%async_computation | async-start | bytes 1835008 | tf_op jit(solution)/shard_map/all_to_all | solution.py:231
where the time goes:
time: 179 us
  blocking collectives  78.7 us (44%)
  waiting for transfers between devices  39.9 us (22%)
  starting transfers between devices  21.7 us (12%)
  other arithmetic  11.5 us (6%)
  local copies, waits for them, and re-layouts  11 us (6%)
  matrix products  10.1 us (6%)
  between operations  5.51 us (3%)
    all_to_all x1, blocking collectives, body(): back = lax.all_to_all(returned, 'ctx', 0, 0, tiled=True)  57.7 us
    all_to_all x1, waiting for transfers between devices, body(): arrived = lax.all_to_all(outbound, 'ctx', 0, 0, tiled=True)  39.9 us
    all_to_all x1, starting transfers between devices, body(): arrived = lax.all_to_all(outbound, 'ctx', 0, 0, tiled=True)  21.7 us
    psum x1, blocking collectives, channel_work(): squares = lax.psum(squares, 'ch')  21 us
    unnamed x22, local copies, waits for them, and re-layouts  8.99 us
  transfers between devices with their start and end apart: 1, of which 1 were waited for; matrix products, arithmetic and copies ran while one was open for 1% of the time, Pallas kernels for 0%

commit v1 on v0

--- a/solution.py
+++ b/solution.py
@@ -9,6 +9,12 @@
 highest = lax.Precision.HIGH
 wide_type = jnp.float32
 narrow_type = jnp.bfloat16
+
+
+def add_all(x, mesh_axis):
+    parts = lax.all_gather(x, mesh_axis, axis=0, tiled=False)
+    total = parts.sum(axis=0)
+    return total
 
 
 def passed_along(array, axis, by):
@@ -185,7 +191,7 @@
         * scale
     )
     squares = jnp.sum(jnp.square(lagged.astype(wide_type))) + jnp.sum(grad_medium * grad_medium)
-    squares = lax.psum(squares, "ch")
+    squares = add_all(squares, "ch")
     medium_high, medium_low = split_wide(grad_medium)
     squares_high, squares_low = split_wide(squares)
     squares_row = jnp.concatenate(

time: 179 us -> 180 us (level)
  local copies, waits for them, and re-layouts: 11 us -> 13.1 us
    psum x1 -> x0, blocking collectives: 21 us -> none  [channel_work(): squares = lax.psum(squares, 'ch')]
    unnamed x0 -> x1, blocking collectives: none -> 20.5 us
    unnamed x22 -> x25, local copies, waits for them, and re-layouts: 8.99 us -> 11 us
  transfers between devices with their start and end apart: 1 -> 1, of which waited for: 1 -> 1; matrix products, arithmetic and copies ran while one was open for 1% -> 2% of each run, Pallas kernels for 0% -> 0%
where the time goes in v1:
time: 180 us; the launch traced here: 179 us
  blocking collectives  78.2 us (43%)
  waiting for transfers between devices  38.6 us (21%)
  starting transfers between devices  21.7 us (12%)
  local copies, waits for them, and re-layouts  13.1 us (7%)
  other arithmetic  12.1 us (7%)
  matrix products  10.1 us (6%)
  between operations  5.53 us (3%)
    all_to_all x1, blocking collectives, body(): back = lax.all_to_all(returned, 'ctx', 0, 0, tiled=True)  57.7 us
    all_to_all x1, waiting for transfers between devices, body(): arrived = lax.all_to_all(outbound, 'ctx', 0, 0, tiled=True)  38.6 us
    all_to_all x1, starting transfers between devices, body(): arrived = lax.all_to_all(outbound, 'ctx', 0, 0, tiled=True)  21.7 us
    unnamed x1, blocking collectives  20.5 us
    unnamed x25, local copies, waits for them, and re-layouts  11 us
  transfers between devices with their start and end apart: 1, of which 1 were waited for; matrix products, arithmetic and copies ran while one was open for 2% of the time, Pallas kernels for 0%

profile of v1, /device:TPU:1, one launch (start us, length us, event | category | flops | bytes accessed | tf_op | source)
XLA Modules:
  0.0 179.3 jit_solution(17139576095074549434)
XLA Ops:
  0.7 1.2 copy.100
  1.8 1.1 copy.99
  3.0 1.1 copy.101
  4.1 1.1 copy.102
  5.6 1.0 pad_maximum_fusion
  6.6 21.7 %all-to-all-start = ((bf16[64,49,128]{2,1,0:T(8,128)(2,1)}), bf16[64,49,128]{2,1,0:T(8,128)(2,1)S(1)}, u32[]{:S(2)}, u32[]{:S(2)}) async-start(bf16[64,49,128]{2,1,0:T(8,128)(2,1)} %pad_maximum_fusion), calls=%async_computation | async-start | bytes 1835008 | tf_op jit(solution)/shard_map/all_to_all | solution.py:237
  28.6 0.4 slice_reduce_fusion
  28.9 0.3 reshape.489
  29.2 1.3 dynamic-slice
  31.5 38.6 %all-to-all-done = bf16[64,49,128]{2,1,0:T(8,128)(2,1)S(1)} async-done(((bf16[64,49,128]{2,1,0:T(8,128)(2,1)}), bf16[64,49,128]{2,1,0:T(8,128)(2,1)S(1)}, u32[]{:S(2)}, u32[]{:S(2)}) %all-to-all-start) | async-done | bytes 802848 | tf_op jit(solution)/shard_map/all_to_all | solution.py:237
  70.9 1.3 convolution_bitcast_fusion
  72.2 0.8 multiply_add_fusion.1
  73.1 2.1 %fusion.12 = f32[32,2,128,128]{2,3,0,1:T(8,128)S(1)} fusion(f32[32,1,128,128]{2,3,1,0:T(8,128)S(1)} %get-tuple-element.38, f32[32,1,128,128]{2,3,1,0:T(8,128)S(1)} %get-tuple-element.37, f32[1,2,128,128]{2,3,0,1:T(8,128)S(1)} %get-tuple-element.64, f32[1,2,128,128]{2,3,0,1:T(8,128)S(1)} %get-tuple-element.71), kind=kOutput, calls=%fused_computation.16 | convolution fusion | flops 1611726848 | bytes 8650752 | tf_op jit(solution)/shard_map/mkab,kjbq->mjaq/dot_general | solution.py:64
  76.3 1.2 multiply_add_fusion.2
  77.8 2.1 %fusion.9 = f32[32,2,128,128]{2,3,1,0:T(8,128)S(1)} fusion(f32[16,2,128,128]{2,3,0,1:T(8,128)S(1)} %maximum_bitcast_fusion.6, f32[16,2,128,128]{2,3,0,1:T(8,128)S(1)} %maximum_bitcast_fusion.5, f32[1,2,128,128]{2,3,1,0:T(8,128)S(1)} %get-tuple-element.72, f32[1,2,128,128]{2,3,1,0:T(8,128)S(1)} %get-tuple-element.63), kind=kOutput, calls=%fused_computation.15 | convolution fusion | flops 1611726848 | bytes 8650752 | tf_op jit(solution)/shard_map/mkab,kjbq->mjaq/dot_general | solution.py:69
  79.9 0.8 multiply_subtract_fusion
  80.7 2.2 %fusion.19 = bf16[64,32,128]{2,0,1:T(8,128)(2,1)S(1)} fusion(f32[32,1,128,128]{2,3,1,0:T(8,128)S(1)} %get-tuple-element.36, f32[32,1,128,128]{2,3,1,0:T(8,128)S(1)} %get-tuple-element.35, f32[1,64,128]{2,1,0:T(8,128)S(1)} %get-tuple-element.79, f32[1,64,128]{2,1,0:T(8,128)S(1)} %get-tuple-element.80), kind=kOutput, calls=%fused_computation.29 | convolution fusion | flops 404242432 | bytes 4784128 | tf_op jit(solution)/shard_map/kna,mkab->nmb/dot_general | solution.py:79
  83.9 2.5 %add_reduce_fusion = f32[128]{0:T(128)S(1)} fusion(f32[128,128]{1,0:T(8,128)S(1)} %convolution_bitcast_fusion.4, f32[128,128]{1,0:T(8,128)S(1)} %convolution_bitcast_fusion.5), kind=kLoop, calls=%fused_computation | loop fusion | flops 16777088 | bytes 131584 | tf_op jit(solution)/shard_map/reduce_sum | solution.py:187
  86.4 0.6 bitcast_convert_fusion
  88.2 0.6 multiply_reduce_fusion
  90.2 0.8 dynamic-update-slice
  90.9 20.5 %all-reduce.4 = f32[8]{0:T(128)S(1)} all-reduce(f32[8]{0:T(128)S(1)} %dynamic-update-slice), channel_id=1, replica_groups=mesh['ctx'=64,'ch'=8] {'ch'}, use_global_device_ids=true, to_apply=%add.4 | all-reduce | flops 8 | bytes 64
  111.4 0.6 reduce_sum.58
  113.4 0.6 copy.118
  114.0 57.7 %all_to_all.10 = bf16[64,52,128]{2,1,0:T(8,128)(2,1)S(1)} all-to-all(bf16[64,52,128]{2,1,0:T(8,128)(2,1)S(1)} %copy.118), channel_id=1, replica_groups=mesh['ctx'=64,'ch'=8] {'ctx'}, dimensions={0} | all-to-all | bytes 1703936 | tf_op jit(solution)/shard_map/all_to_all | solution.py:250
  172.0 0.8 copy.121
  172.9 0.8 copy.124
  173.8 0.8 copy.123
  174.6 0.8 copy.122
  175.6 0.7 add_reduce_fusion.1
  176.9 0.6 copy.173
  177.5 0.7 fusion.83
  (56 shorter events, 6.3 us)
Async XLA Ops:
  0.6 27.7 %copy-start = (bf16[128,64]{0,1:T(8,128)(2,1)S(1)}, bf16[128,64]{0,1:T(8,128)(2,1)}, u32[]{:S(2)}) copy-start(bf16[128,64]{0,1:T(8,128)(2,1)} %param.12) | copy-start | bytes 49156
  0.6 4.6 %copy-start.1 = (bf16[128,1024]{1,0:T(8,128)(2,1)S(1)}, bf16[128,1024]{1,0:T(8,128)(2,1)}, u32[]{:S(2)}) copy-start(bf16[128,1024]{1,0:T(8,128)(2,1)} %param.8) | copy-start | bytes 786436
  0.7 4.7 %copy-start.2 = (bf16[128,64]{0,1:T(8,128)(2,1)S(1)}, bf16[128,64]{0,1:T(8,128)(2,1)}, u32[]{:S(2)}) copy-start(bf16[128,64]{0,1:T(8,128)(2,1)} %param.13) | copy-start | bytes 49156
  6.6 63.5 %all-to-all-start = ((bf16[64,49,128]{2,1,0:T(8,128)(2,1)}), bf16[64,49,128]{2,1,0:T(8,128)(2,1)S(1)}, u32[]{:S(2)}, u32[]{:S(2)}) async-start(bf16[64,49,128]{2,1,0:T(8,128)(2,1)} %pad_maximum_fusion), calls=%async_computation | async-start | bytes 1835008 | tf_op jit(solution)/shard_map/all_to_all | solution.py:237
